TPU v7x, 512 devices: a whole 4x4x16 slice. The times are simulated.
512 devices in a mesh: seq: 64 (over z, y), tp: 4 (over x), dp: 2 (over core).
Axes of the slice: x: 4, y: 4, z: 16, core: 2. Of those that a mesh axis runs over, the one named last changes fastest.
Arguments:
- inputs: bfloat16 [16384, 1280], P(('dp', 'seq'), 'tp'), parts along dimension 0, may hold values from -6 to 6
- out_grads: bfloat16 [16384, 1280], P(('dp', 'seq'), 'tp'), parts along dimension 0, may hold values from -6 to 6
- norm_gain: float32 [1280], replicated, may hold values from 0.1 to 1.9
- w_query: bfloat16 [640, 1280], P('tp'), may hold values from -0.15625 to 0.15625
- w_key: bfloat16 [640, 1280], P('tp'), may hold values from -0.15625 to 0.15625
- w_value: bfloat16 [640, 1280], P('tp'), may hold values from -0.15625 to 0.15625
- w_output: bfloat16 [640, 1280], P('tp'), may hold values from -0.25 to 0.25
- query_scale: float32 [80], replicated, may hold values from -4 to 4
- offsets: int32 [64], replicated, may hold values from 0 to 63, each once
Outputs:
- input_grads: bfloat16 [16384, 1280], P(('dp', 'seq'), 'tp'), parts along dimension 0
There are 2 independent parts, one for each index of `dp`. A program takes and returns all parts, laid end to end along the dimension named above; an argument that names none is the same for every part. Nothing has to cross between parts.
Inputs may be any that keep to these rules, and one draw needn't show every extreme that they name: `offsets`: each number appears exactly once.
All inputs are finite; a program needn't handle non-finite values.
Results may differ from a plain program's by a relative error of at most 0.007.
The roundings to bfloat16 on the way count: a program that leaves them out, or rounds other values in their place, can miss the bound.
Values may be sent and summed in bfloat16 or wider, within the bound.
No kernel may reach another device: no remote copies, remote signals or barrier semaphores. Data moves between devices by JAX's collectives and lax.ppermute only.
A program may use at most 64 MiB of HBM per device.

v0:
```python
import math
import jax
import jax.numpy as jnp
from jax import lax
from jax.sharding import PartitionSpec as P

PIECE = 128
scale_base = 1.4426950408889634
masked_score = -1e30
norm_eps = 1e-06


def positions_of(offsets, first_row, piece_rows, block_len):
    row_index = first_row + lax.iota(jnp.int32, piece_rows)
    shard_ids = row_index // block_len
    one_hot = (shard_ids[:, None] == lax.iota(jnp.int32, offsets.shape[0])[None, :]).astype(
        jnp.int32
    )
    return jnp.sum(one_hot * offsets[None, :], axis=1) * block_len + row_index % block_len


def column_scale(query_scale, head_count):
    head_width = query_scale.shape[0]
    factor = scale_base / math.sqrt(head_width) * jax.nn.softplus(query_scale)
    return jnp.tile(factor, head_count)


def split_heads(values, head_count):
    return values.reshape(values.shape[0], head_count, values.shape[1] // head_count)


def over_blocks(running, pieces, step_fn):
    piece_rows = pieces[0].shape[0]
    block_size = math.gcd(piece_rows, 512)

    def visit_block(number, state_now):
        first_row = number * block_size
        block_parts = tuple(
            (lax.dynamic_slice_in_dim(piece, first_row, block_size, 0) for piece in pieces)
        )
        return step_fn(state_now, block_parts, first_row)

    return lax.fori_loop(0, piece_rows // block_size, visit_block, running)


def per_device(
    inputs, out_grads, norm_gain, w_query, w_key, w_value, w_output, query_scale, offsets
):
    row_count = inputs.shape[0]
    width_here = inputs.shape[1]
    head_width = query_scale.shape[0]
    heads_here = w_query.shape[0] // head_width
    contract = (((1,), (1,)), ((), ()))
    full_inputs, full_grads = (
        lax.all_gather(inputs, "tp", axis=1, tiled=True),
        lax.all_gather(out_grads, "tp", axis=1, tiled=True),
    )
    full_width = full_inputs.shape[1]
    widened = full_inputs.astype(jnp.float32)
    inverse = lax.rsqrt(jnp.mean(widened * widened, axis=1, keepdims=True) + norm_eps)
    normed = (widened * inverse * norm_gain[None, :]).astype(jnp.bfloat16)
    factor = column_scale(query_scale, heads_here)
    queries = (
        lax.dot_general(normed, w_query, contract, preferred_element_type=jnp.float32)
        * factor[None, :]
    ).astype(jnp.bfloat16)
    key_rows = lax.dot_general(normed, w_key, contract, preferred_element_type=jnp.float32).astype(
        jnp.bfloat16
    )
    values = lax.dot_general(normed, w_value, contract, preferred_element_type=jnp.float32).astype(
        jnp.bfloat16
    )
    head_grads = lax.dot_general(
        full_grads, w_output, contract, preferred_element_type=jnp.float32
    ).astype(jnp.bfloat16)
    seq_index = lax.axis_index("seq")
    own_positions = positions_of(offsets, seq_index * row_count, row_count, PIECE)
    query_heads = split_heads(queries, heads_here)
    grad_heads = split_heads(head_grads, heads_here)
    key_heads = split_heads(key_rows, heads_here)
    value_heads = split_heads(values, heads_here)

    def peak_step(running, block_parts, first_row):
        key_part = block_parts[0]
        key_place = positions_of(offsets, first_row, key_part.shape[0], PIECE)
        row_peak, summed = running
        raw_scores = jnp.einsum(
            "qhd,khd->hqk",
            query_heads,
            split_heads(key_part, heads_here),
            preferred_element_type=jnp.float32,
        )
        visible = key_place[None, None, :] <= own_positions[None, :, None]
        masked = jnp.where(visible, raw_scores, masked_score)
        fresh_peak = jnp.maximum(row_peak, jnp.max(masked, axis=2))
        fresh_terms = jnp.where(visible, jnp.exp(masked - fresh_peak[:, :, None]), 0.0)
        summed = summed * jnp.exp(row_peak - fresh_peak) + jnp.sum(fresh_terms, axis=2)
        return (fresh_peak, summed)

    def make_grad_step(log_total):

        def grad_step(running, block_parts, first_row):
            key_part, value_part = block_parts
            key_place = positions_of(offsets, first_row, key_part.shape[0], PIECE)
            row_delta, first_sum, second_sum = running
            key_heads_part = split_heads(key_part, heads_here)
            raw_scores = jnp.einsum(
                "qhd,khd->hqk", query_heads, key_heads_part, preferred_element_type=jnp.float32
            )
            visible = key_place[None, None, :] <= own_positions[None, :, None]
            attend = jnp.exp(jnp.where(visible, raw_scores - log_total[:, :, None], masked_score))
            grad_probs = jnp.einsum(
                "qhd,khd->hqk",
                grad_heads,
                split_heads(value_part, heads_here),
                preferred_element_type=jnp.float32,
            )
            weighted = attend * grad_probs
            row_delta = row_delta + jnp.sum(weighted, axis=2)
            first_sum = first_sum + jnp.einsum(
                "hqk,khd->hqd",
                weighted.astype(jnp.bfloat16),
                key_heads_part,
                preferred_element_type=jnp.float32,
            )
            second_sum = second_sum + jnp.einsum(
                "hqk,khd->hqd",
                attend.astype(jnp.bfloat16),
                key_heads_part,
                preferred_element_type=jnp.float32,
            )
            return (row_delta, first_sum, second_sum)

        return grad_step

    peak_start = (
        jnp.full((heads_here, row_count), masked_score, jnp.float32),
        jnp.zeros((heads_here, row_count), jnp.float32),
    )
    grad_start = (
        jnp.zeros((heads_here, row_count), jnp.float32),
        jnp.zeros((heads_here, row_count, head_width), jnp.float32),
        jnp.zeros((heads_here, row_count, head_width), jnp.float32),
    )
    row_peak, summed = over_blocks(
        peak_start, (lax.all_gather(key_rows, "seq", axis=0, tiled=True),), peak_step
    )
    log_total = row_peak + jnp.log(summed)
    grad_step = make_grad_step(log_total)
    row_delta, first_sum, second_sum = over_blocks(
        grad_start,
        (
            lax.all_gather(key_rows, "seq", axis=0, tiled=True),
            lax.all_gather(values, "seq", axis=0, tiled=True),
        ),
        grad_step,
    )
    query_grad = first_sum - row_delta[:, :, None] * second_sum
    query_grad = jnp.transpose(query_grad, (1, 0, 2)).reshape(row_count, heads_here * head_width)
    query_done = (query_grad * factor[None, :]).astype(jnp.bfloat16)
    log_all, delta_all = (
        lax.all_gather(log_total.T, "seq", axis=0, tiled=True),
        lax.all_gather(row_delta.T, "seq", axis=0, tiled=True),
    )

    def key_step(running, block_parts, first_row):
        query_part, grad_part = block_parts
        piece_rows = query_part.shape[0]
        query_place = positions_of(offsets, first_row, piece_rows, PIECE)
        log_part = lax.dynamic_slice_in_dim(log_all, first_row, piece_rows, 0).T
        delta_part = lax.dynamic_slice_in_dim(delta_all, first_row, piece_rows, 0).T
        key_grad, value_grad = running
        query_heads_part = split_heads(query_part, heads_here)
        grad_heads_part = split_heads(grad_part, heads_here)
        raw_scores = jnp.einsum(
            "qhd,khd->hqk", query_heads_part, key_heads, preferred_element_type=jnp.float32
        )
        visible = own_positions[None, None, :] <= query_place[None, :, None]
        attend = jnp.exp(jnp.where(visible, raw_scores - log_part[:, :, None], masked_score))
        grad_probs = jnp.einsum(
            "qhd,khd->hqk", grad_heads_part, value_heads, preferred_element_type=jnp.float32
        )
        score_grad = (attend * (grad_probs - delta_part[:, :, None])).astype(jnp.bfloat16)
        key_grad = key_grad + jnp.einsum(
            "hqk,qhd->khd", score_grad, query_heads_part, preferred_element_type=jnp.float32
        )
        value_grad = value_grad + jnp.einsum(
            "hqk,qhd->khd",
            attend.astype(jnp.bfloat16),
            grad_heads_part,
            preferred_element_type=jnp.float32,
        )
        return (key_grad, value_grad)

    key_start = (
        jnp.zeros((row_count, heads_here, head_width), jnp.float32),
        jnp.zeros((row_count, heads_here, head_width), jnp.float32),
    )
    key_grad, value_grad = over_blocks(
        key_start,
        (
            lax.all_gather(queries, "seq", axis=0, tiled=True),
            lax.all_gather(head_grads, "seq", axis=0, tiled=True),
        ),
        key_step,
    )
    key_done = key_grad.reshape(row_count, heads_here * head_width).astype(jnp.bfloat16)
    value_done = value_grad.reshape(row_count, heads_here * head_width).astype(jnp.bfloat16)
    back_sum = jnp.dot(query_done, w_query, preferred_element_type=jnp.float32)
    back_sum = back_sum + jnp.dot(key_done, w_key, preferred_element_type=jnp.float32)
    back_sum = back_sum + jnp.dot(value_done, w_value, preferred_element_type=jnp.float32)
    start_col = lax.axis_index("tp") * width_here
    total_back = lax.psum(back_sum, "tp")
    scaled = total_back * norm_gain[None, :]
    row_dot = jnp.sum(widened * scaled, axis=1, keepdims=True)
    branch = inverse * scaled - widened * inverse * inverse * inverse * row_dot / full_width
    result = out_grads.astype(jnp.float32) + lax.dynamic_slice_in_dim(
        branch, start_col, width_here, 1
    )
    return result.astype(jnp.bfloat16)


def solution(mesh):
    return jax.shard_map(
        per_device,
        mesh=mesh,
        in_specs=(
            P(("dp", "seq"), "tp"),
            P(("dp", "seq"), "tp"),
            P(),
            P("tp", None),
            P("tp", None),
            P("tp", None),
            P("tp", None),
            P(),
            P(),
        ),
        out_specs=P(("dp", "seq"), "tp"),
        check_vma=False,
    )
```

profile of v0, /device:TPU:8, one launch (start us, length us, event | category | flops | bytes accessed | tf_op | source)
XLA Modules:
  0.0 678.4 jit_solution(6673104376951234624)
XLA Ops:
  6.6 13.1 %all_gather.25 = bf16[128,1280]{0,1:T(8,128)(2,1)S(1)} all-gather(bf16[128,320]{0,1:T(8,128)(2,1)} %param.15), channel_id=1, replica_groups=mesh['seq'=64,'tp'=4,'dp'=2] {'tp'}, dimensions={1}, use_global_device_ids=true | all-gather | bytes 409600 | tf_op jit(solution)/shard_map/all_gather | solution.py:55
  19.9 2.1 convolution_convert_fusion.2
  22.0 2.1 convolution_convert_fusion.1
  25.4 12.4 %all_gather.28 = bf16[128,1280]{0,1:T(8,128)(2,1)S(1)} all-gather(bf16[128,320]{0,1:T(8,128)(2,1)S(1)} %copy-done.6), channel_id=1, replica_groups=mesh['seq'=64,'tp'=4,'dp'=2] {'tp'}, dimensions={1}, use_global_device_ids=true | all-gather | bytes 409600 | tf_op jit(solution)/shard_map/all_gather | solution.py:56
  39.0 125.1 %all-gather.5.cloned.1.call-done = bf16[8192,160]{0,1:T(8,128)(2,1)} async-done(((bf16[128,160]{0,1:T(8,128)(2,1)}), bf16[8192,160]{0,1:T(8,128)(2,1)}) %all-gather.5.cloned.1.call-update) | async-done | bytes 2621456 | tf_op jit(solution)/shard_map/all_gather | solution.py:153
  164.1 39.6 %while.56 = (s32[]{:T(128)}, f32[2,128]{1,0:T(2,128)S(1)}, f32[2,128]{1,0:T(2,128)S(1)}, s32[64]{0:T(128)S(1)}, s32[128]{0:T(128)S(1)}, /*index=5*/bf16[8192,160...) while((s32[]{:T(128)}, f32[2,128]{1,0:T(2,128)S(1)}, ...), condition=%wide.region_6.7_spmd.clone, body=%wide.region_2.6_spmd.clone.sunk | while | flops 21806852 | bytes 1804210 | solution.py:43
  165.3 1.1 fusion.103
  167.8 1.1 fusion.103
  170.2 1.1 fusion.103
  172.7 1.1 fusion.103
  175.2 1.1 fusion.103
  177.7 1.1 fusion.103
  180.1 1.1 fusion.103
  182.6 1.1 fusion.103
  185.1 1.1 fusion.103
  187.6 1.1 fusion.103
  190.1 1.1 fusion.103
  192.5 1.1 fusion.103
  195.0 1.1 fusion.103
  197.5 1.1 fusion.103
  200.0 1.1 fusion.103
  202.4 1.1 fusion.103
  203.7 97.4 %all-gather.7.cloned.1.call-done = bf16[8192,160]{0,1:T(8,128)(2,1)} async-done(((bf16[128,160]{0,1:T(8,128)(2,1)}), bf16[8192,160]{0,1:T(8,128)(2,1)}) %all-gather.7.cloned.1.call-update) | async-done | bytes 2621456 | tf_op jit(solution)/shard_map/all_gather | solution.py:154
  301.1 50.2 %while.57 = (s32[]{:T(128)}, f32[2,128]{1,0:T(2,128)S(1)}, f32[2,128,80]{1,2,0:T(8,128)S(1)}, f32[2,128,80]{1,2,0:T(8,128)S(1)}, s32[64]{0:T(128)S(1)}, /*index=...) while((s32[]{:T(128)}, f32[2,128]{1,0:T(2,128)S(1)}, ...), condition=%wide.region_10.11_spmd.clone, body=%wide.region_7.10_spmd.clone.sunk | while | flops 84933376 | bytes 3966931 | solution.py:43
  314.9 1.1 fusion.115
  351.3 80.1 %all_gather.32 = f32[8192,2]{0,1:T(2,128)S(1)} all-gather(f32[128,2]{0,1:T(2,128)S(1)} %bitcast.134), channel_id=1, replica_groups=mesh['seq'=64,'tp'=4,'dp'=2] {'seq'}, dimensions={0}, use_global_device_ids=true | all-gather | bytes 66560 | tf_op jit(solution)/shard_map/all_gather | solution.py:163
  431.4 80.0 %all_gather.30 = f32[8192,2]{0,1:T(2,128)S(1)} all-gather(f32[128,2]{0,1:T(2,128)S(1)} %bitcast.133), channel_id=1, replica_groups=mesh['seq'=64,'tp'=4,'dp'=2] {'seq'}, dimensions={0}, use_global_device_ids=true | all-gather | bytes 66560 | tf_op jit(solution)/shard_map/all_gather | solution.py:162
  511.4 63.3 %all-gather.11.cloned.1.call-done = bf16[8192,160]{0,1:T(8,128)(2,1)} async-done(((bf16[128,160]{0,1:T(8,128)(2,1)}), bf16[8192,160]{0,1:T(8,128)(2,1)}) %all-gather.11.cloned.1.call-update) | async-done | bytes 2621456 | tf_op jit(solution)/shard_map/all_gather | solution.py:203
  574.8 37.7 %while.58 = (s32[]{:T(128)}, f32[128,2,80]{0,2,1:T(8,128)S(1)}, f32[128,2,80]{0,2,1:T(8,128)S(1)}, bf16[8192,160]{0,1:T(8,128)(2,1)}, s32[128]{0:T(128)S(1)}, /*...) while((s32[]{:T(128)}, f32[128,2,80]{0,2,1:T(8,128)S(1)}, ...), condition=%wide.region_13.14_spmd.clone, body=%wide.region_11.13_spmd.clone.sunk | while | flops 84933120 | bytes 3462102 | solution.py:43
  613.5 1.2 convolution_add_fusion.2
  614.7 55.1 %all-reduce.2.cloned.1.call-done = f32[128,1280]{0,1:T(8,128)} async-done(((f32[128,1280]{0,1:T(8,128)}), f32[128,1280]{0,1:T(8,128)}) %all-reduce.2.cloned.1.call-update) | async-done | bytes 655376 | tf_op jit(solution)/shard_map/psum | solution.py:213
  669.8 1.3 fusion.33
  (505 shorter events, 110.3 us)
Async XLA Ops:
  6.5 17.7 %copy-start = (bf16[160,1280]{1,0:T(8,128)(2,1)S(1)}, bf16[160,1280]{1,0:T(8,128)(2,1)}, u32[]{:S(2)}) copy-start(bf16[160,1280]{1,0:T(8,128)(2,1)} %param.18) | copy-start | bytes 1228804
  6.5 17.7 %copy-start.9 = (f32[1280]{0:T(1024)S(1)}, f32[1280]{0:T(1024)}, u32[]{:S(2)}) copy-start(f32[1280]{0:T(1024)} %param.17) | copy-start | bytes 15364
  6.5 17.6 %copy-start.10 = (f32[80]{0:T(128)S(1)}, f32[80]{0:T(128)}, u32[]{:S(2)}) copy-start(f32[80]{0:T(128)} %param.22) | copy-start | bytes 964
  6.5 18.9 %copy-start.6 = (bf16[128,320]{0,1:T(8,128)(2,1)S(1)}, bf16[128,320]{0,1:T(8,128)(2,1)}, u32[]{:S(2)}) copy-start(bf16[128,320]{0,1:T(8,128)(2,1)} %param.16) | copy-start | bytes 245764
  6.5 31.3 %copy-start.5 = (bf16[160,1280]{1,0:T(8,128)(2,1)S(1)}, bf16[160,1280]{1,0:T(8,128)(2,1)}, u32[]{:S(2)}) copy-start(bf16[160,1280]{1,0:T(8,128)(2,1)} %param.21) | copy-start | bytes 1228804
  6.5 32.3 %copy-start.7 = (s32[64]{0:T(128)S(1)}, s32[64]{0:T(128)}, u32[]{:S(2)}) copy-start(s32[64]{0:T(128)} %param.23) | copy-start | bytes 772
  6.6 157.5 %all-gather.5.cloned.1.call-start = ((), (), s32[]{:S(2)}) async-start(), calls=%async_computation | async-start | bytes 2662400 | tf_op jit(solution)/shard_map/all_gather | solution.py:153
  22.0 279.1 %all-gather.7.cloned.1.call-start = ((), (), s32[]{:S(2)}) async-start(), calls=%async_computation.1 | async-start | bytes 2662400 | tf_op jit(solution)/shard_map/all_gather | solution.py:154
  24.1 487.3 %all-gather.9.cloned.1.call-start = ((), (), s32[]{:S(2)}) async-start(), calls=%async_computation.2 | async-start | bytes 2662400 | tf_op jit(solution)/shard_map/all_gather | solution.py:202
  25.4 549.4 %all-gather.11.cloned.1.call-start = ((), (), s32[]{:S(2)}) async-start(), calls=%async_computation.3 | async-start | bytes 2662400 | tf_op jit(solution)/shard_map/all_gather | solution.py:203
  38.7 631.1 %all-reduce.2.cloned.1.call-start = ((), (), s32[]{:S(2)}) async-start(), calls=%async_computation.4 | async-start | bytes 1310720 | tf_op jit(solution)/shard_map/psum | solution.py:213
  164.1 137.0 %copy-start.1 = (bf16[128,160]{0,1:T(8,128)(2,1)S(1)}, bf16[128,160]{0,1:T(8,128)(2,1)}, u32[]{:S(2)}) copy-start(bf16[128,160]{0,1:T(8,128)(2,1)} %convolution_convert_fusion) | copy-start | bytes 122884
  301.1 273.7 %copy-start.2 = (bf16[128,160]{0,1:T(8,128)(2,1)S(1)}, bf16[128,160]{0,1:T(8,128)(2,1)}, u32[]{:S(2)}) copy-start(bf16[128,160]{0,1:T(8,128)(2,1)} %convolution_convert_fusion.1) | copy-start | bytes 122884
  301.1 273.7 %copy-start.8 = (bf16[128,160]{0,1:T(8,128)(2,1)S(1)}, bf16[128,160]{0,1:T(8,128)(2,1)}, u32[]{:S(2)}) copy-start(bf16[128,160]{0,1:T(8,128)(2,1)} %convolution_convert_fusion.2) | copy-start | bytes 122884
  574.8 38.2 %copy-start.3 = (bf16[160,1280]{1,0:T(8,128)(2,1)S(1)}, bf16[160,1280]{1,0:T(8,128)(2,1)}, u32[]{:S(2)}) copy-start(bf16[160,1280]{1,0:T(8,128)(2,1)} %param.19) | copy-start | bytes 1228804
  612.5 1.0 copy-start.4
Sparse Core Ops, SparseCore 0:
  22.1 141.9 all-gather.4
  167.0 134.0 all-gather.6
  304.0 133.7 all-gather.8
  440.6 134.1 all-gather.10
  614.8 54.9 all-reduce.1
where the time goes:
time: 682 us; the launch traced here: 678 us
  waiting for transfers between devices  341 us (50%)
  blocking collectives  186 us (27%)
  matrix products  69.4 us (10%)
  local copies, waits for them, and re-layouts  48.2 us (7%)
  other arithmetic  17.4 us (3%)
  between operations  13.4 us (2%)
    all_gather x1, waiting for transfers between devices, per_device(): lax.all_gather(key_rows, 'seq', axis=0, tiled=True)  125 us
    all_gather x1, waiting for transfers between devices, per_device(): lax.all_gather(values, 'seq', axis=0, tiled=True)  97.4 us
    all_gather x1, blocking collectives, per_device(): lax.all_gather(row_delta.T, 'seq', axis=0, tiled=True)  80.1 us
    all_gather x1, blocking collectives, per_device(): lax.all_gather(log_total.T, 'seq', axis=0, tiled=True)  80 us
    all_gather x1, waiting for transfers between devices, per_device(): lax.all_gather(head_grads, 'seq', axis=0, tiled=True)  63.3 us
    psum x1, waiting for transfers between devices, per_device(): total_back = lax.psum(back_sum, 'tp')  55.1 us
    dynamic_slice x48, local copies, waits for them, and re-layouts, visit_block(): lax.dynamic_slice_in_dim(piece, first_row, block_size, 0)  47.7 us
    dot_general x16, matrix products, peak_step(): jnp.einsum('qhd,khd->hqk', query_heads, split_heads(key_part, heads_here)...  17.2 us
  transfers between devices with their start and end apart: 5, of which 4 were waited for; matrix products, arithmetic and copies ran while one was open for 14% of the time, Pallas kernels for 0%

commit v1 on v0

--- a/solution.py
+++ b/solution.py
@@ -210,7 +210,8 @@
     back_sum = back_sum + jnp.dot(key_done, w_key, preferred_element_type=jnp.float32)
     back_sum = back_sum + jnp.dot(value_done, w_value, preferred_element_type=jnp.float32)
     start_col = lax.axis_index("tp") * width_here
-    total_back = lax.psum(back_sum, "tp")
+    opened = lax.all_gather(back_sum, "tp")
+    total_back = jnp.sum(opened, 0)
     scaled = total_back * norm_gain[None, :]
     row_dot = jnp.sum(widened * scaled, axis=1, keepdims=True)
     branch = inverse * scaled - widened * inverse * inverse * inverse * row_dot / full_width

time: 682 us -> 667 us (0.978)
  the two profiles are of different devices: /device:TPU:8 before, /device:TPU:1 now
where the time goes in v1:
time: 667 us; the launch traced here: 664 us
  waiting for transfers between devices  360 us (54%)
  blocking collectives  152 us (23%)
  matrix products  69.1 us (10%)
  local copies, waits for them, and re-layouts  48.6 us (7%)
  other arithmetic  18.2 us (3%)
  between operations  13.4 us (2%)
    all_gather x1, waiting for transfers between devices, per_device(): lax.all_gather(key_rows, 'seq', axis=0, tiled=True)  122 us
    all_gather x1, waiting for transfers between devices, per_device(): lax.all_gather(values, 'seq', axis=0, tiled=True)  97.4 us
    all_gather x1, waiting for transfers between devices, per_device(): lax.all_gather(head_grads, 'seq', axis=0, tiled=True)  92.3 us
    all_gather x1, blocking collectives, per_device(): lax.all_gather(log_total.T, 'seq', axis=0, tiled=True)  65.6 us
    all_gather x1, blocking collectives, per_device(): lax.all_gather(row_delta.T, 'seq', axis=0, tiled=True)  65.5 us
    all_gather x1, waiting for transfers between devices, per_device(): opened = lax.all_gather(back_sum, 'tp')  48.3 us
    dynamic_slice x48, local copies, waits for them, and re-layouts, visit_block(): lax.dynamic_slice_in_dim(piece, first_row, block_size, 0)  47.7 us
    dot_general x16, matrix products, peak_step(): jnp.einsum('qhd,khd->hqk', query_heads, split_heads(key_part, heads_here)...  17.2 us
  transfers between devices with their start and end apart: 5, of which 4 were waited for; matrix products, arithmetic and copies ran while one was open for 14% of the time, Pallas kernels for 0%

profile of v1, /device:TPU:1, one launch (start us, length us, event | category | flops | bytes accessed | tf_op | source)
XLA Modules:
  0.0 664.2 jit_solution(12008940505054289163)
XLA Ops:
  6.6 11.0 %all_gather.31 = bf16[128,1280]{0,1:T(8,128)(2,1)S(1)} all-gather(bf16[128,320]{0,1:T(8,128)(2,1)} %param.15), channel_id=1, replica_groups=mesh['seq'=64,'tp'=4,'dp'=2] {'tp'}, dimensions={1}, use_global_device_ids=true | all-gather | bytes 409600 | tf_op jit(solution)/shard_map/all_gather | solution.py:55
  17.8 2.1 convolution_convert_fusion.2
  20.0 2.1 convolution_convert_fusion.1
  23.4 9.5 %all_gather.34 = bf16[128,1280]{0,1:T(8,128)(2,1)S(1)} all-gather(bf16[128,320]{0,1:T(8,128)(2,1)S(1)} %copy-done.6), channel_id=1, replica_groups=mesh['seq'=64,'tp'=4,'dp'=2] {'tp'}, dimensions={1}, use_global_device_ids=true | all-gather | bytes 409600 | tf_op jit(solution)/shard_map/all_gather | solution.py:56
  34.0 121.6 %all-gather.7.cloned.1.call-done = bf16[8192,160]{0,1:T(8,128)(2,1)} async-done(((bf16[128,160]{0,1:T(8,128)(2,1)}), bf16[8192,160]{0,1:T(8,128)(2,1)}) %all-gather.7.cloned.1.call-update) | async-done | bytes 2621456 | tf_op jit(solution)/shard_map/all_gather | solution.py:153
  155.6 39.6 %while.56 = (s32[]{:T(128)}, f32[2,128]{1,0:T(2,128)S(1)}, f32[2,128]{1,0:T(2,128)S(1)}, s32[64]{0:T(128)S(1)}, s32[128]{0:T(128)S(1)}, /*index=5*/bf16[8192,160...) while((s32[]{:T(128)}, f32[2,128]{1,0:T(2,128)S(1)}, ...), condition=%wide.region_6.7_spmd.clone, body=%wide.region_2.6_spmd.clone.sunk | while | flops 21806852 | bytes 1804210 | solution.py:43
  156.9 1.1 fusion.103
  159.3 1.1 fusion.103
  161.8 1.1 fusion.103
  164.3 1.1 fusion.103
  166.8 1.1 fusion.103
  169.2 1.1 fusion.103
  171.7 1.1 fusion.103
  174.2 1.1 fusion.103
  176.7 1.1 fusion.103
  179.1 1.1 fusion.103
  181.6 1.1 fusion.103
  184.1 1.1 fusion.103
  186.6 1.1 fusion.103
  189.0 1.1 fusion.103
  191.5 1.1 fusion.103
  194.0 1.1 fusion.103
  195.3 97.4 %all-gather.9.cloned.1.call-done = bf16[8192,160]{0,1:T(8,128)(2,1)} async-done(((bf16[128,160]{0,1:T(8,128)(2,1)}), bf16[8192,160]{0,1:T(8,128)(2,1)}) %all-gather.9.cloned.1.call-update) | async-done | bytes 2621456 | tf_op jit(solution)/shard_map/all_gather | solution.py:154
  292.6 50.2 %while.57 = (s32[]{:T(128)}, f32[2,128]{1,0:T(2,128)S(1)}, f32[2,128,80]{1,2,0:T(8,128)S(1)}, f32[2,128,80]{1,2,0:T(8,128)S(1)}, s32[64]{0:T(128)S(1)}, /*index=...) while((s32[]{:T(128)}, f32[2,128]{1,0:T(2,128)S(1)}, ...), condition=%wide.region_10.11_spmd.clone, body=%wide.region_7.10_spmd.clone.sunk | while | flops 84933376 | bytes 3966931 | solution.py:43
  315.9 1.1 fusion.115
  342.9 65.5 %all_gather.38 = f32[8192,2]{0,1:T(2,128)S(1)} all-gather(f32[128,2]{0,1:T(2,128)S(1)} %bitcast.136), channel_id=1, replica_groups=mesh['seq'=64,'tp'=4,'dp'=2] {'seq'}, dimensions={0}, use_global_device_ids=true | all-gather | bytes 66560 | tf_op jit(solution)/shard_map/all_gather | solution.py:163
  408.4 65.6 %all_gather.36 = f32[8192,2]{0,1:T(2,128)S(1)} all-gather(f32[128,2]{0,1:T(2,128)S(1)} %bitcast.135), channel_id=1, replica_groups=mesh['seq'=64,'tp'=4,'dp'=2] {'seq'}, dimensions={0}, use_global_device_ids=true | all-gather | bytes 66560 | tf_op jit(solution)/shard_map/all_gather | solution.py:162
  474.0 92.3 %all-gather.13.cloned.1.call-done = bf16[8192,160]{0,1:T(8,128)(2,1)} async-done(((bf16[128,160]{0,1:T(8,128)(2,1)}), bf16[8192,160]{0,1:T(8,128)(2,1)}) %all-gather.13.cloned.1.call-update) | async-done | bytes 2621456 | tf_op jit(solution)/shard_map/all_gather | solution.py:203
  566.4 37.7 %while.58 = (s32[]{:T(128)}, f32[128,2,80]{0,2,1:T(8,128)S(1)}, f32[128,2,80]{0,2,1:T(8,128)S(1)}, bf16[8192,160]{0,1:T(8,128)(2,1)}, s32[128]{0:T(128)S(1)}, /*...) while((s32[]{:T(128)}, f32[128,2,80]{0,2,1:T(8,128)S(1)}, ...), condition=%wide.region_13.14_spmd.clone, body=%wide.region_11.13_spmd.clone.sunk | while | flops 84933120 | bytes 3462102 | solution.py:43
  605.0 1.1 convolution_add_fusion.2
  606.2 48.3 %all-gather.15.cloned.1.call-done = f32[512,1280]{1,0:T(8,128)} async-done(((f32[128,1280]{1,0:T(8,128)}), f32[512,1280]{1,0:T(8,128)}) %all-gather.15.cloned.1.call-update) | async-done | bytes 2621456 | tf_op jit(solution)/shard_map/all_gather | solution.py:213
  654.5 2.0 reduce_sum.118
  (507 shorter events, 110.8 us)
Async XLA Ops:
  6.5 15.7 %copy-start = (bf16[160,1280]{1,0:T(8,128)(2,1)S(1)}, bf16[160,1280]{1,0:T(8,128)(2,1)}, u32[]{:S(2)}) copy-start(bf16[160,1280]{1,0:T(8,128)(2,1)} %param.18) | copy-start | bytes 1228804
  6.5 15.7 %copy-start.9 = (f32[1280]{0:T(1024)S(1)}, f32[1280]{0:T(1024)}, u32[]{:S(2)}) copy-start(f32[1280]{0:T(1024)} %param.17) | copy-start | bytes 15364
  6.5 15.6 %copy-start.10 = (f32[80]{0:T(128)S(1)}, f32[80]{0:T(128)}, u32[]{:S(2)}) copy-start(f32[80]{0:T(128)} %param.22) | copy-start | bytes 964
  6.5 16.8 %copy-start.6 = (bf16[128,320]{0,1:T(8,128)(2,1)S(1)}, bf16[128,320]{0,1:T(8,128)(2,1)}, u32[]{:S(2)}) copy-start(bf16[128,320]{0,1:T(8,128)(2,1)} %param.16) | copy-start | bytes 245764
  6.5 26.3 %copy-start.5 = (bf16[160,1280]{1,0:T(8,128)(2,1)S(1)}, bf16[160,1280]{1,0:T(8,128)(2,1)}, u32[]{:S(2)}) copy-start(bf16[160,1280]{1,0:T(8,128)(2,1)} %param.21) | copy-start | bytes 1228804
  6.5 27.4 %copy-start.7 = (s32[64]{0:T(128)S(1)}, s32[64]{0:T(128)}, u32[]{:S(2)}) copy-start(s32[64]{0:T(128)} %param.23) | copy-start | bytes 772
  6.6 149.1 %all-gather.7.cloned.1.call-start = ((), (), s32[]{:S(2)}) async-start(), calls=%async_computation | async-start | bytes 2662400 | tf_op jit(solution)/shard_map/all_gather | solution.py:153
  19.9 272.7 %all-gather.9.cloned.1.call-start = ((), (), s32[]{:S(2)}) async-start(), calls=%async_computation.1 | async-start | bytes 2662400 | tf_op jit(solution)/shard_map/all_gather | solution.py:154
  22.0 452.0 %all-gather.11.cloned.1.call-start = ((), (), s32[]{:S(2)}) async-start(), calls=%async_computation.2 | async-start | bytes 2662400 | tf_op jit(solution)/shard_map/all_gather | solution.py:202
  23.3 543.1 %all-gather.13.cloned.1.call-start = ((), (), s32[]{:S(2)}) async-start(), calls=%async_computation.3 | async-start | bytes 2662400 | tf_op jit(solution)/shard_map/all_gather | solution.py:203
  33.8 620.7 %all-gather.15.cloned.1.call-start = ((), (), s32[]{:S(2)}) async-start(), calls=%async_computation.4 | async-start | bytes 3276800 | tf_op jit(solution)/shard_map/all_gather | solution.py:213
  155.6 137.0 %copy-start.1 = (bf16[128,160]{0,1:T(8,128)(2,1)S(1)}, bf16[128,160]{0,1:T(8,128)(2,1)}, u32[]{:S(2)}) copy-start(bf16[128,160]{0,1:T(8,128)(2,1)} %convolution_convert_fusion) | copy-start | bytes 122884
  292.6 273.7 %copy-start.2 = (bf16[128,160]{0,1:T(8,128)(2,1)S(1)}, bf16[128,160]{0,1:T(8,128)(2,1)}, u32[]{:S(2)}) copy-start(bf16[128,160]{0,1:T(8,128)(2,1)} %convolution_convert_fusion.1) | copy-start | bytes 122884
  292.6 273.7 %copy-start.8 = (bf16[128,160]{0,1:T(8,128)(2,1)S(1)}, bf16[128,160]{0,1:T(8,128)(2,1)}, u32[]{:S(2)}) copy-start(bf16[128,160]{0,1:T(8,128)(2,1)} %convolution_convert_fusion.2) | copy-start | bytes 122884
  566.4 38.1 %copy-start.3 = (bf16[160,1280]{1,0:T(8,128)(2,1)S(1)}, bf16[160,1280]{1,0:T(8,128)(2,1)}, u32[]{:S(2)}) copy-start(bf16[160,1280]{1,0:T(8,128)(2,1)} %param.19) | copy-start | bytes 1228804
  604.0 1.0 copy-start.4
Sparse Core Ops, SparseCore 0:
  20.0 135.5 all-gather.6
  158.6 134.0 all-gather.8
  295.6 134.9 all-gather.10
  433.3 132.9 all-gather.12
  606.3 48.1 all-gather.14
